TPU v7x, 32 devices: a whole 2x2x4 slice. The times are simulated.
32 devices in a mesh: dp: 4 (over z), expert: 8 (over y, x, core).
Axes of the slice: x: 2, y: 2, z: 4, core: 2. Of those that a mesh axis runs over, the one named last changes fastest.
Arguments:
- tokens: bfloat16 [384, 4096], P('expert', 'dp'), may hold values from -6 to 6
- out_grad: bfloat16 [384, 4096], P('expert', 'dp'), may hold values from -6 to 6
- expert_ids: int32 [384, 8], P('expert'), may hold values from 0 to 63, all different within a row; in each aligned block of 48 rows (0 to 47, 48 to 95, ...) at most 12 rows name the same one
- route_weights: float32 [384, 8], P('expert'), may hold values from 0.05 to 1
- gate_weight: bfloat16 [64, 4096, 768], P('expert', 'dp'), may hold values from -0.09375 to 0.09375
- up_weight: bfloat16 [64, 4096, 768], P('expert', 'dp'), may hold values from -0.09375 to 0.09375
- down_weight: bfloat16 [64, 768, 4096], P('expert', None, 'dp'), may hold values from -0.21875 to 0.21875
Outputs:
- layer_out: bfloat16 [384, 4096], P('expert', 'dp')
- grad_tokens: bfloat16 [384, 4096], P('expert', 'dp')
- gate_grad: bfloat16 [64, 4096, 768], P('expert', 'dp')
- up_grad: bfloat16 [64, 4096, 768], P('expert', 'dp')
- down_grad: bfloat16 [64, 768, 4096], P('expert', None, 'dp')
Inputs may be any that keep to these rules, and one draw needn't show every extreme that they name: `expert_ids`: each row names 8 different experts. In the 48 rows of one index of the expert axis no expert is named more than 12 times, and in every draw some expert is named exactly 12 times there.
All inputs are finite; a program needn't handle non-finite values.
Results may differ from a plain program's by a relative error of at most 0.029.
Values may be sent and summed in bfloat16 or wider, within the bound.
No kernel may reach another device: no remote copies, remote signals or barrier semaphores. Data moves between devices by JAX's collectives and lax.ppermute only.
A program may use at most 128 MiB of HBM per device.

v0:
```python
import jax
import jax.numpy as jnp
from jax import lax
from jax.sharding import PartitionSpec as P


def swiglu_parts(gate_sum, up_sum, back_sum):
    logistic = jax.nn.sigmoid(gate_sum)
    activated = gate_sum * logistic
    hidden = (activated * up_sum).astype(jnp.bfloat16)
    gate_delta = (back_sum * up_sum * logistic * (1.0 + gate_sum * (1.0 - logistic))).astype(
        jnp.bfloat16
    )
    up_delta = (back_sum * activated).astype(jnp.bfloat16)
    return (hidden, gate_delta, up_delta)


def split_f32(value):
    high = value.astype(jnp.bfloat16)
    rest = value - high.astype(jnp.float32)
    middle = rest.astype(jnp.bfloat16)
    low = (rest - middle.astype(jnp.float32)).astype(jnp.bfloat16)
    return (high, middle, low)


def local(tokens, out_grad, expert_ids, route_weights, gate_weight, up_weight, down_weight):
    token_count, width_dev = tokens.shape
    per_token = expert_ids.shape[1]
    local_experts = gate_weight.shape[0]
    hidden_units = gate_weight.shape[2]
    sources = lax.axis_size("expert")
    experts = local_experts * sources
    capacity = 2 * token_count * per_token // experts
    slot_count = token_count * per_token
    me = lax.axis_index("expert")
    high, middle, low = split_f32(route_weights)
    route_cols = 4 * per_token
    pad_cols = -route_cols % 128
    packed = jnp.concatenate(
        [
            tokens,
            out_grad,
            expert_ids.astype(jnp.bfloat16),
            high,
            middle,
            low,
            jnp.zeros((token_count, pad_cols), jnp.bfloat16),
        ],
        axis=1,
    )
    gathered = lax.all_to_all(
        jnp.broadcast_to(packed[None], (sources,) + packed.shape).reshape(
            sources * token_count, packed.shape[1]
        ),
        "expert",
        split_axis=0,
        concat_axis=0,
        tiled=True,
    )
    feats = gathered[:, : 2 * width_dev]
    route_all = gathered[:, 2 * width_dev : 2 * width_dev + route_cols].astype(jnp.float32)
    ids_all = route_all[:, :per_token].astype(jnp.int32)
    w_all = (
        route_all[:, per_token : 2 * per_token]
        + route_all[:, 2 * per_token : 3 * per_token]
        + route_all[:, 3 * per_token :]
    )
    all_tokens = sources * token_count
    flat_all = ids_all.reshape(sources, slot_count)
    position = jnp.arange(slot_count, dtype=jnp.int32)
    earlier = (flat_all[:, None, :] == flat_all[:, :, None]) & (
        position[None, None, :] < position[None, :, None]
    )
    rank_all = jnp.sum(earlier.astype(jnp.int32), axis=2)
    local_e = flat_all - me * local_experts
    is_local = (local_e >= 0) & (local_e < local_experts)
    src = jnp.arange(sources, dtype=jnp.int32)[:, None]
    row_count = local_experts * sources * capacity
    row_of = jnp.where(is_local, (local_e * sources + src) * capacity + rank_all, row_count)
    row_of = row_of.reshape(sources * slot_count)
    token_of = jnp.arange(sources * slot_count, dtype=jnp.int32) // per_token
    target = jnp.arange(row_count, dtype=jnp.int32)
    hit = target[:, None] == row_of[None, :]
    holder = jnp.sum(jnp.where(hit, token_of[None, :] + 1, 0), axis=1) - 1
    row_weight = jnp.sum(jnp.where(hit, w_all.reshape(-1)[None, :], 0.0), axis=1)
    select = (holder[:, None] == jnp.arange(all_tokens, dtype=jnp.int32)[None, :]).astype(
        jnp.bfloat16
    )
    picked = jnp.dot(select, feats, preferred_element_type=jnp.float32)
    x_in = picked[:, :width_dev].astype(jnp.bfloat16)
    dy_in = (row_weight[:, None] * picked[:, width_dev:]).astype(jnp.bfloat16)
    x_in = x_in.reshape(local_experts, sources * capacity, width_dev)
    dy_in = dy_in.reshape(local_experts, sources * capacity, width_dev)
    gate_part = jnp.einsum(
        "jrd,jdf->jrf", x_in, gate_weight, preferred_element_type=jnp.float32
    ).astype(jnp.bfloat16)
    up_part = jnp.einsum(
        "jrd,jdf->jrf", x_in, up_weight, preferred_element_type=jnp.float32
    ).astype(jnp.bfloat16)
    front = jnp.concatenate([gate_part, up_part], axis=2).reshape(row_count, 2 * hidden_units)
    front_sums = lax.psum_scatter(front, "dp", scatter_dimension=0, tiled=True)
    back_part = jnp.einsum(
        "jrd,jfd->jrf", dy_in, down_weight, preferred_element_type=jnp.float32
    ).astype(jnp.bfloat16)
    dp_count = lax.axis_size("dp")
    back_blocks = lax.all_to_all(
        back_part.reshape(row_count, hidden_units), "dp", split_axis=0, concat_axis=0, tiled=True
    )
    back_sums = jnp.sum(
        back_blocks.reshape(dp_count, row_count // dp_count, hidden_units).astype(jnp.float32),
        axis=0,
    )
    front_sums = front_sums.astype(jnp.float32)
    hidden, gate_delta, up_delta = swiglu_parts(
        front_sums[:, :hidden_units], front_sums[:, hidden_units:], back_sums
    )
    hidden = lax.all_gather(hidden, "dp", axis=0, tiled=True)
    deltas = lax.all_gather(
        jnp.concatenate([gate_delta, up_delta], axis=1), "dp", axis=0, tiled=True
    )
    expert_shape = (local_experts, sources, capacity, hidden_units)
    hidden = hidden.reshape(expert_shape)
    gate_delta = deltas[:, :hidden_units].reshape(expert_shape)
    up_delta = deltas[:, hidden_units:].reshape(expert_shape)
    rows_shape = (local_experts, sources * capacity, hidden_units)
    buffer_rows = experts * capacity
    expert_out = jnp.einsum(
        "jrf,jfd->jrd", hidden.reshape(rows_shape), down_weight, preferred_element_type=jnp.float32
    ).astype(jnp.bfloat16)
    expert_out = expert_out.reshape(local_experts, sources, capacity, width_dev).transpose(
        1, 0, 2, 3
    )
    out_back = lax.all_to_all(
        expert_out.reshape(buffer_rows, width_dev),
        "expert",
        split_axis=0,
        concat_axis=0,
        tiled=True,
    )
    down_grad = jnp.einsum(
        "jrf,jrd->jfd", hidden.reshape(rows_shape), dy_in, preferred_element_type=jnp.float32
    ).astype(jnp.bfloat16)
    expert_back = (
        jnp.einsum(
            "jrf,jdf->jrd",
            gate_delta.reshape(rows_shape),
            gate_weight,
            preferred_element_type=jnp.float32,
        )
        + jnp.einsum(
            "jrf,jdf->jrd",
            up_delta.reshape(rows_shape),
            up_weight,
            preferred_element_type=jnp.float32,
        )
    ).astype(jnp.bfloat16)
    expert_back = expert_back.reshape(local_experts, sources, capacity, width_dev).transpose(
        1, 0, 2, 3
    )
    grad_back = lax.all_to_all(
        expert_back.reshape(buffer_rows, width_dev),
        "expert",
        split_axis=0,
        concat_axis=0,
        tiled=True,
    )
    gate_grad = jnp.einsum(
        "jrd,jrf->jdf", x_in, gate_delta.reshape(rows_shape), preferred_element_type=jnp.float32
    ).astype(jnp.bfloat16)
    up_grad = jnp.einsum(
        "jrd,jrf->jdf", x_in, up_delta.reshape(rows_shape), preferred_element_type=jnp.float32
    ).astype(jnp.bfloat16)
    flat_ids = expert_ids.reshape(slot_count)
    earlier_local = (flat_ids[None, :] == flat_ids[:, None]) & (
        position[None, :] < position[:, None]
    )
    slot_rank = jnp.sum(earlier_local.astype(jnp.int32), axis=1)
    slot_place = (flat_ids * capacity + slot_rank).reshape(token_count, per_token)
    picked_out = jnp.take(out_back, slot_place, axis=0).astype(jnp.float32)
    layer_out = jnp.sum(picked_out * route_weights[:, :, None], axis=1).astype(jnp.bfloat16)
    picked_back = jnp.take(grad_back, slot_place, axis=0).astype(jnp.float32)
    grad_tokens = jnp.sum(picked_back, axis=1).astype(jnp.bfloat16)
    return (layer_out, grad_tokens, gate_grad, up_grad, down_grad)


def solution(mesh):
    in_specs = (
        P("expert", "dp"),
        P("expert", "dp"),
        P("expert", None),
        P("expert", None),
        P("expert", "dp", None),
        P("expert", "dp", None),
        P("expert", None, "dp"),
    )
    out_specs = (
        P("expert", "dp"),
        P("expert", "dp"),
        P("expert", "dp", None),
        P("expert", "dp", None),
        P("expert", None, "dp"),
    )
    return jax.shard_map(local, mesh=mesh, in_specs=in_specs, out_specs=out_specs, check_vma=False)
```

profile of v0, /device:TPU:0, one launch (start us, length us, event | category | flops | bytes accessed | tf_op | source)
XLA Modules:
  0.0 272.1 jit_solution(667128261609481006)
XLA Ops:
  7.2 0.7 convert_element_type.82
  7.9 0.8 subtract_convert_fusion
  9.0 1.0 concatenate.9
  10.1 1.3 broadcast_in_dim.60
  11.3 5.2 %all-to-all-start = ((bf16[8,48,2176]{2,1,0:T(8,128)(2,1)}), bf16[8,48,2176]{2,1,0:T(8,128)(2,1)S(1)}, u32[]{:S(2)}, u32[]{:S(2)}) async-start(bf16[8,48,2176]{2,1,0:T(8,128)(2,1)} %broadcast_in_dim.60), calls=%async_computation | async-start | bytes 3342336 | tf_op jit(solution)/shard_map/all_to_all | solution.py:51
  16.6 22.0 %all-to-all-done = bf16[8,48,2176]{2,1,0:T(8,128)(2,1)S(1)} async-done(((bf16[8,48,2176]{2,1,0:T(8,128)(2,1)}), bf16[8,48,2176]{2,1,0:T(8,128)(2,1)S(1)}, u32[]{:S(2)}, u32[]{:S(2)}) %all-to-all-start) | async-done | bytes 1671200 | tf_op jit(solution)/shard_map/all_to_all | solution.py:51
  38.7 0.2 slice_add_fusion
  39.4 1.6 convert_reduce_fusion
  41.0 1.2 select_reduce_fusion.1
  42.3 1.8 fusion.1
  44.1 3.2 %copy-done.1 = f32[768,2048]{1,0:T(8,128)} copy-done((f32[768,2048]{1,0:T(8,128)}, f32[768,2048]{1,0:T(8,128)S(1)}, u32[]{:S(2)}) %copy-start.1) | copy-done | bytes 6291480
  47.3 0.2 slice.90
  47.5 1.6 copy-done
  49.1 2.0 convolution_convert_fusion.5
  51.1 6.6 %convolution_convert_fusion.6 = bf16[8,96,768]{2,1,0:T(8,128)(2,1)S(1)} fusion(bf16[8,96,1024]{2,1,0:T(8,128)(2,1)S(1)} %bitcast.45, bf16[8,1024,768]{2,1,0:T(8,128)(2,1)} %param.13), kind=kOutput, calls=%fused_computation.21 | convolution fusion | flops 1208549376 | bytes 15335424 | tf_op jit(solution)/shard_map/jrd,jdf->jrf/dot_general | solution.py:94
  57.7 1.6 pad_maximum_fusion
  59.3 0.2 all-gather.3.cloned.1.call-start
  59.7 1.2 select_reduce_fusion
  60.9 2.1 fusion
  63.0 9.6 %convolution_convert_fusion.4 = bf16[8,96,768]{2,1,0:T(8,128)(2,1)S(1)} fusion(bf16[8,96,1024]{2,1,0:T(8,128)(2,1)S(1)} %bitcast.50, bf16[8,768,1024]{2,1,0:T(8,128)(2,1)} %param.15), kind=kOutput, calls=%fused_computation.19 | convolution fusion | flops 1208549376 | bytes 15335424 | tf_op jit(solution)/shard_map/jrd,jfd->jrf/dot_general | solution.py:102
  72.6 58.2 %all_to_all.42 = bf16[4,192,768]{2,1,0:T(8,128)(2,1)S(1)} all-to-all(bf16[4,192,768]{2,1,0:T(8,128)(2,1)S(1)} %bitcast.63), channel_id=1, replica_groups=mesh['dp'=4,'expert'=8] {'dp'}, dimensions={0} | all-to-all | bytes 2359296 | tf_op jit(solution)/shard_map/all_to_all | solution.py:106
  131.0 1.2 convert_element_type.93
  132.2 1.1 multiply_convert_fusion.1
  133.3 0.9 pad_maximum_fusion.1
  134.2 28.9 %all-gather.3.cloned.1.call-done = bf16[768,768]{1,0:T(8,128)(2,1)} async-done(((bf16[192,768]{1,0:T(8,128)(2,1)}), bf16[768,768]{1,0:T(8,128)(2,1)}) %all-gather.3.cloned.1.call-update) | async-done | bytes 1179664 | tf_op jit(solution)/shard_map/all_gather | solution.py:117
  163.1 7.1 %convolution_convert_fusion.3 = bf16[8,96,1024]{2,1,0:T(8,128)(2,1)S(1)} fusion(bf16[8,96,768]{2,1,0:T(8,128)(2,1)} %bitcast.64, bf16[8,768,1024]{2,1,0:T(8,128)(2,1)} %param.15), kind=kOutput, calls=%fused_computation.15 | convolution fusion | flops 1208745984 | bytes 15335424 | tf_op jit(solution)/shard_map/jrf,jfd->jrd/dot_general | solution.py:127
  170.2 0.9 copy.68
  171.1 0.9 copy.69
  171.9 2.0 copy.70
  173.9 3.9 %all-to-all-start.1 = ((bf16[8,96,1024]{2,1,0:T(8,128)(2,1)}), bf16[8,96,1024]{2,1,0:T(8,128)(2,1)S(1)}, u32[]{:S(2)}, u32[]{:S(2)}) async-start(bf16[8,96,1024]{2,1,0:T(8,128)(2,1)} %copy.70), calls=%async_computation.2 | async-start | bytes 3145728 | tf_op jit(solution)/shard_map/all_to_all | solution.py:133
  178.2 0.2 convert_reduce_fusion.2
  178.9 10.0 %convolution_convert_fusion = bf16[8,768,1024]{2,1,0:T(8,128)(2,1)} fusion(bf16[8,96,768]{2,1,0:T(8,128)(2,1)} %bitcast.65, bf16[8,96,1024]{2,1,0:T(8,128)(2,1)} %bitcast.51), kind=kOutput, calls=%fused_computation.5 | convolution fusion | flops 1214251008 | bytes 15335424 | tf_op jit(solution)/shard_map/jrf,jrd->jfd/dot_general | solution.py:140
  188.9 9.9 %all-to-all-done.1 = bf16[8,96,1024]{2,1,0:T(8,128)(2,1)S(1)} async-done(((bf16[8,96,1024]{2,1,0:T(8,128)(2,1)}), bf16[8,96,1024]{2,1,0:T(8,128)(2,1)S(1)}, u32[]{:S(2)}, u32[]{:S(2)}) %all-to-all-start.1) | async-done | bytes 1572896 | tf_op jit(solution)/shard_map/all_to_all | solution.py:133
  198.8 2.7 gather_fusion
  201.4 12.9 %all-gather.5.cloned.1.call-done = bf16[768,1536]{1,0:T(8,128)(2,1)} async-done(((bf16[192,1536]{1,0:T(8,128)(2,1)}), bf16[768,1536]{1,0:T(8,128)(2,1)}) %all-gather.5.cloned.1.call-update) | async-done | bytes 2359312 | tf_op jit(solution)/shard_map/all_gather | solution.py:118
  214.3 1.8 fusion.11
  216.1 9.3 %fusion.12 = f32[8,96,1024]{2,1,0:T(8,128)S(1)} fusion(bf16[8,96,768]{2,1,0:T(8,128)(2,1)S(1)} %bitcast.52, bf16[8,1024,768]{2,1,0:T(8,128)(2,1)} %param.13), kind=kOutput, calls=%fused_computation.58 | convolution fusion | flops 1207959552 | bytes 16908288 | tf_op jit(solution)/shard_map/jrf,jdf->jrd/dot_general | solution.py:144
  225.5 8.5 %add_convert_fusion = bf16[8,96,1024]{2,1,0:T(8,128)(2,1)S(1)} fusion(f32[8,96,1024]{2,1,0:T(8,128)S(1)} %fusion.12, bf16[8,96,768]{2,1,0:T(8,128)(2,1)S(1)} %bitcast.54, bf16[8,1024,768]{2,1,0:T(8,128)(2,1)} %param.14), kind=kOutput, calls=%fused_computation.12 | convolution fusion | flops 1209532416 | bytes 18481152 | tf_op jit(solution)/shard_map/jrf,jdf->jrd/dot_general | solution.py:150
  233.9 0.9 copy.74
  234.8 0.9 copy.75
  235.7 2.0 copy.76
  237.7 3.8 %all-to-all-start.3 = ((bf16[8,96,1024]{2,1,0:T(8,128)(2,1)}), bf16[8,96,1024]{2,1,0:T(8,128)(2,1)S(1)}, u32[]{:S(2)}, u32[]{:S(2)}) async-start(bf16[8,96,1024]{2,1,0:T(8,128)(2,1)} %copy.76), calls=%async_computation.4 | async-start | bytes 3145728 | tf_op jit(solution)/shard_map/all_to_all | solution.py:160
  241.6 2.4 multiply_reduce_fusion
  244.0 8.0 %convolution_convert_fusion.1 = bf16[8,1024,768]{2,1,0:T(8,128)(2,1)} fusion(bf16[8,96,1024]{2,1,0:T(8,128)(2,1)S(1)} %bitcast.46, bf16[8,96,768]{2,1,0:T(8,128)(2,1)} %bitcast.55), kind=kOutput, calls=%fused_computation.6 | convolution fusion | flops 1214251008 | bytes 15335424 | tf_op jit(solution)/shard_map/jrd,jrf->jdf/dot_general | solution.py:170
  252.0 6.6 %convolution_convert_fusion.2 = bf16[8,1024,768]{2,1,0:T(8,128)(2,1)} fusion(bf16[8,96,1024]{2,1,0:T(8,128)(2,1)S(1)} %bitcast.47, bf16[8,96,768]{2,1,0:T(8,128)(2,1)S(1)} %bitcast.53), kind=kOutput, calls=%fused_computation.7 | convolution fusion | flops 1214251008 | bytes 15335424 | tf_op jit(solution)/shard_map/jrd,jrf->jdf/dot_general | solution.py:167
  258.6 3.8 %all-to-all-done.3 = bf16[8,96,1024]{2,1,0:T(8,128)(2,1)S(1)} async-done(((bf16[8,96,1024]{2,1,0:T(8,128)(2,1)}), bf16[8,96,1024]{2,1,0:T(8,128)(2,1)S(1)}, u32[]{:S(2)}, u32[]{:S(2)}) %all-to-all-start.3) | async-done | bytes 1572896 | tf_op jit(solution)/shard_map/all_to_all | solution.py:160
  262.4 2.1 gather_fusion.1
  264.5 1.1 fusion.3
  (49 shorter events, 2.2 us)
Async XLA Ops:
  11.3 27.3 %all-to-all-start = ((bf16[8,48,2176]{2,1,0:T(8,128)(2,1)}), bf16[8,48,2176]{2,1,0:T(8,128)(2,1)S(1)}, u32[]{:S(2)}, u32[]{:S(2)}) async-start(bf16[8,48,2176]{2,1,0:T(8,128)(2,1)} %broadcast_in_dim.60), calls=%async_computation | async-start | bytes 3342336 | tf_op jit(solution)/shard_map/all_to_all | solution.py:51
  16.5 114.5 %reduce-scatter.2.cloned.1.call-start = ((), (), s32[]{:S(2)}) async-start(), calls=%async_computation.5 | async-start | bytes 2949120 | tf_op jit(solution)/shard_map/reduce_scatter | solution.py:101
  42.2 6.9 %copy-start = (bf16[8,1024,768]{2,1,0:T(8,128)(2,1)S(1)}, bf16[8,1024,768]{2,1,0:T(8,128)(2,1)}, u32[]{:S(2)}) copy-start(bf16[8,1024,768]{2,1,0:T(8,128)(2,1)} %param.14) | copy-start | bytes 37748740
  44.1 3.2 %copy-start.1 = (f32[768,2048]{1,0:T(8,128)}, f32[768,2048]{1,0:T(8,128)S(1)}, u32[]{:S(2)}) copy-start(f32[768,2048]{1,0:T(8,128)S(1)} %fusion.1) | copy-start | bytes 18874372
  59.3 103.8 %all-gather.3.cloned.1.call-start = ((), (), s32[]{:S(2)}) async-start(), calls=%async_computation.6 | async-start | bytes 1474560 | tf_op jit(solution)/shard_map/all_gather | solution.py:117
  63.0 9.6 %copy-start.2 = (bf16[768,1024]{1,0:T(8,128)(2,1)}, bf16[768,1024]{1,0:T(8,128)(2,1)S(1)}, u32[]{:S(2)}) copy-start(bf16[768,1024]{1,0:T(8,128)(2,1)S(1)} %fusion) | copy-start | bytes 4718596
  133.3 81.0 %all-gather.5.cloned.1.call-start = ((), (), s32[]{:S(2)}) async-start(), calls=%async_computation.7 | async-start | bytes 2949120 | tf_op jit(solution)/shard_map/all_gather | solution.py:118
  173.9 3.9 %copy-start.7 = (f32[48,8]{0,1:T(8,128)S(1)}, f32[48,8]{0,1:T(8,128)}, u32[]{:S(2)}) copy-start(f32[48,8]{0,1:T(8,128)} %param.12) | copy-start | bytes 4612
  173.9 4.0 %copy-start.6 = (s32[48,8]{0,1:T(8,128)S(1)}, s32[48,8]{0,1:T(8,128)}, u32[]{:S(2)}) copy-start(s32[48,8]{0,1:T(8,128)} %param.11) | copy-start | bytes 4612
  173.9 24.8 %all-to-all-start.1 = ((bf16[8,96,1024]{2,1,0:T(8,128)(2,1)}), bf16[8,96,1024]{2,1,0:T(8,128)(2,1)S(1)}, u32[]{:S(2)}, u32[]{:S(2)}) async-start(bf16[8,96,1024]{2,1,0:T(8,128)(2,1)} %copy.70), calls=%async_computation.2 | async-start | bytes 3145728 | tf_op jit(solution)/shard_map/all_to_all | solution.py:133
  216.1 9.3 %copy-start.3 = (bf16[768,768]{1,0:T(8,128)(2,1)}, bf16[768,768]{1,0:T(8,128)(2,1)S(1)}, u32[]{:S(2)}) copy-start(bf16[768,768]{1,0:T(8,128)(2,1)S(1)} %get-tuple-element.9) | copy-start | bytes 3538948
  216.1 9.3 %copy-start.5 = (bf16[768,768]{1,0:T(8,128)(2,1)}, bf16[768,768]{1,0:T(8,128)(2,1)S(1)}, u32[]{:S(2)}) copy-start(bf16[768,768]{1,0:T(8,128)(2,1)S(1)} %get-tuple-element.8) | copy-start | bytes 3538948
  237.7 24.7 %all-to-all-start.3 = ((bf16[8,96,1024]{2,1,0:T(8,128)(2,1)}), bf16[8,96,1024]{2,1,0:T(8,128)(2,1)S(1)}, u32[]{:S(2)}, u32[]{:S(2)}) async-start(bf16[8,96,1024]{2,1,0:T(8,128)(2,1)} %copy.76), calls=%async_computation.4 | async-start | bytes 3145728 | tf_op jit(solution)/shard_map/all_to_all | solution.py:160
  244.0 8.0 %copy-start.4 = (bf16[768,768]{1,0:T(8,128)(2,1)S(1)}, bf16[768,768]{1,0:T(8,128)(2,1)}, u32[]{:S(2)}) copy-start(bf16[768,768]{1,0:T(8,128)(2,1)} %copy-done.3) | copy-start | bytes 3538948
Sparse Core Ops, SparseCore 0:
  59.4 66.0 reduce-scatter.1
  133.4 29.6 all-gather.2
  164.7 49.5 all-gather.4
where the time goes:
time: 273 us; the launch traced here: 272 us
  waiting for transfers between devices  77.5 us (28%)
  matrix products  69.5 us (25%)
  blocking collectives  58.2 us (21%)
  local copies, waits for them, and re-layouts  23 us (8%)
  other arithmetic  16.6 us (6%)
  between operations  14.1 us (5%)
  starting transfers between devices  13.2 us (5%)
    all_to_all x1, blocking collectives, local(): lax.all_to_all(back_part.reshape(row_count, hidden_units), 'dp', split_ax...  58.2 us
    all_gather x1, waiting for transfers between devices, local(): hidden = lax.all_gather(hidden, 'dp', axis=0, tiled=True)  28.9 us
    all_to_all x1, waiting for transfers between devices, local(): lax.all_to_all(jnp.broadcast_to(packed[None], (sources,) + packed.shape)....  22 us
    all_gather x1, waiting for transfers between devices, local(): lax.all_gather(jnp.concatenate([gate_delta, up_delta], axis=1), 'dp', axi...  12.9 us
    dot_general x1, matrix products, local(): jnp.einsum('jrf,jrd->jfd', hidden.reshape(rows_shape), dy_in, preferred_e...  10 us
    all_to_all x1, waiting for transfers between devices, local(): lax.all_to_all(expert_out.reshape(buffer_rows, width_dev), 'expert', spli...  9.89 us
    dot_general x1, matrix products, local(): jnp.einsum('jrd,jfd->jrf', dy_in, down_weight, preferred_element_type=jnp...  9.56 us
    dot_general x1, matrix products, local(): jnp.einsum('jrf,jdf->jrd', gate_delta.reshape(rows_shape), gate_weight, p...  9.3 us
  transfers between devices with their start and end apart: 6, of which 5 were waited for; matrix products, arithmetic and copies ran while one was open for 20% of the time, Pallas kernels for 0%

commit v1 on v0

--- a/solution.py
+++ b/solution.py
@@ -2,6 +2,24 @@
 import jax.numpy as jnp
 from jax import lax
 from jax.sharding import PartitionSpec as P
+
+
+def laid_out(parts, dim):
+    shape = list(parts.shape[1:])
+    shape[dim] *= parts.shape[0]
+    return jnp.moveaxis(parts, 0, dim).reshape(shape)
+
+
+def doubled(x, axis):
+    count = lax.axis_size(axis)
+    blocks = x[None]
+    for level in range(count.bit_length() - 1):
+        stride = 1 << level
+        other = lax.ppermute(blocks, axis, [(i, i ^ stride) for i in range(count)])
+        both = jnp.stack([blocks, other])
+        upper = lax.axis_index(axis) >> level & 1
+        blocks = jnp.where(upper == 0, both, both[::-1]).reshape(-1, *x.shape)
+    return blocks
 
 
 def swiglu_parts(gate_sum, up_sum, back_sum):
@@ -114,7 +132,7 @@
     hidden, gate_delta, up_delta = swiglu_parts(
         front_sums[:, :hidden_units], front_sums[:, hidden_units:], back_sums
     )
-    hidden = lax.all_gather(hidden, "dp", axis=0, tiled=True)
+    hidden = laid_out(doubled(hidden, "dp"), 0)
     deltas = lax.all_gather(
         jnp.concatenate([gate_delta, up_delta], axis=1), "dp", axis=0, tiled=True
     )

time: 273 us -> 298 us (1.092)
  waiting for transfers between devices: 77.5 us -> 97.9 us
  starting transfers between devices: 13.2 us -> 17.4 us
    ppermute x0 -> x2, waiting for transfers between devices: none -> 62.1 us  [doubled(): other = lax.ppermute(blocks, axis, [(i, i ^ stride) for i in range(count)])]
    all_gather x1 -> x0, waiting for transfers between devices: 28.9 us -> none  [local(): hidden = lax.all_gather(hidden, 'dp', axis=0, tiled=True)]
    all_gather x1, waiting for transfers between devices: 12.9 us -> 0.01 us  [local(): lax.all_gather(jnp.concatenate([gate_delta, up_delta], axis=1), 'dp', axi...]
    ppermute x0 -> x2, starting transfers between devices: none -> 3.47 us  [doubled(): other = lax.ppermute(blocks, axis, [(i, i ^ stride) for i in range(count)])]
  transfers between devices with their start and end apart: 6 -> 7, of which waited for: 5 -> 5; matrix products, arithmetic and copies ran while one was open for 20% -> 19% of each run, Pallas kernels for 0% -> 0%
where the time goes in v1:
time: 298 us; the launch traced here: 297 us
  waiting for transfers between devices  97.9 us (33%)
  matrix products  69.6 us (23%)
  blocking collectives  58.2 us (20%)
  local copies, waits for them, and re-layouts  23 us (8%)
  starting transfers between devices  17.4 us (6%)
  other arithmetic  16.4 us (6%)
  between operations  14.4 us (5%)
    ppermute x2, waiting for transfers between devices, doubled(): other = lax.ppermute(blocks, axis, [(i, i ^ stride) for i in range(count)])  62.1 us
    all_to_all x1, blocking collectives, local(): lax.all_to_all(back_part.reshape(row_count, hidden_units), 'dp', split_ax...  58.2 us
    all_to_all x1, waiting for transfers between devices, local(): lax.all_to_all(jnp.broadcast_to(packed[None], (sources,) + packed.shape)....  22 us
    all_to_all x1, waiting for transfers between devices, local(): lax.all_to_all(expert_out.reshape(buffer_rows, width_dev), 'expert', spli...  10.1 us
    dot_general x1, matrix products, local(): jnp.einsum('jrf,jrd->jfd', hidden.reshape(rows_shape), dy_in, preferred_e...  10 us
    dot_general x1, matrix products, local(): jnp.einsum('jrd,jfd->jrf', dy_in, down_weight, preferred_element_type=jnp...  9.56 us
    dot_general x1, matrix products, local(): jnp.einsum('jrf,jdf->jrd', gate_delta.reshape(rows_shape), gate_weight, p...  9.31 us
    dot_general x1, matrix products, local(): jnp.einsum('jrf,jdf->jrd', up_delta.reshape(rows_shape), up_weight, prefe...  8.47 us
  transfers between devices with their start and end apart: 7, of which 5 were waited for; matrix products, arithmetic and copies ran while one was open for 19% of the time, Pallas kernels for 0%

profile of v1, /device:TPU:0, one launch (start us, length us, event | category | flops | bytes accessed | tf_op | source)
XLA Modules:
  0.0 296.9 jit_solution(2263988803650777588)
XLA Ops:
  7.2 0.7 convert_element_type.82
  7.9 0.8 subtract_convert_fusion
  9.0 1.0 concatenate.9
  10.1 1.3 broadcast_in_dim.63
  11.3 5.2 %all-to-all-start = ((bf16[8,48,2176]{2,1,0:T(8,128)(2,1)}), bf16[8,48,2176]{2,1,0:T(8,128)(2,1)S(1)}, u32[]{:S(2)}, u32[]{:S(2)}) async-start(bf16[8,48,2176]{2,1,0:T(8,128)(2,1)} %broadcast_in_dim.63), calls=%async_computation | async-start | bytes 3342336 | tf_op jit(solution)/shard_map/all_to_all | solution.py:69
  16.6 22.0 %all-to-all-done = bf16[8,48,2176]{2,1,0:T(8,128)(2,1)S(1)} async-done(((bf16[8,48,2176]{2,1,0:T(8,128)(2,1)}), bf16[8,48,2176]{2,1,0:T(8,128)(2,1)S(1)}, u32[]{:S(2)}, u32[]{:S(2)}) %all-to-all-start) | async-done | bytes 1671200 | tf_op jit(solution)/shard_map/all_to_all | solution.py:69
  39.4 1.6 convert_reduce_fusion
  41.0 1.2 select_reduce_fusion.1
  42.2 1.8 fusion.1
  44.1 3.2 %copy-done.1 = f32[768,2048]{1,0:T(8,128)} copy-done((f32[768,2048]{1,0:T(8,128)}, f32[768,2048]{1,0:T(8,128)S(1)}, u32[]{:S(2)}) %copy-start.1) | copy-done | bytes 6291480
  47.3 0.2 slice.90
  47.5 1.6 copy-done
  49.1 2.0 convolution_convert_fusion.5
  51.1 6.6 %convolution_convert_fusion.6 = bf16[8,96,768]{2,1,0:T(8,128)(2,1)S(1)} fusion(bf16[8,96,1024]{2,1,0:T(8,128)(2,1)S(1)} %bitcast.53, bf16[8,1024,768]{2,1,0:T(8,128)(2,1)} %param.13), kind=kOutput, calls=%fused_computation.22 | convolution fusion | flops 1208549376 | bytes 15335424 | tf_op jit(solution)/shard_map/jrd,jdf->jrf/dot_general | solution.py:112
  57.7 1.6 pad_maximum_fusion
  59.7 1.2 select_reduce_fusion
  60.9 2.1 fusion
  63.0 9.6 %convolution_convert_fusion.4 = bf16[8,96,768]{2,1,0:T(8,128)(2,1)S(1)} fusion(bf16[8,96,1024]{2,1,0:T(8,128)(2,1)S(1)} %bitcast.58, bf16[8,768,1024]{2,1,0:T(8,128)(2,1)} %param.15), kind=kOutput, calls=%fused_computation.20 | convolution fusion | flops 1208549376 | bytes 15335424 | tf_op jit(solution)/shard_map/jrd,jfd->jrf/dot_general | solution.py:120
  72.6 58.2 %all_to_all.42 = bf16[4,192,768]{2,1,0:T(8,128)(2,1)S(1)} all-to-all(bf16[4,192,768]{2,1,0:T(8,128)(2,1)S(1)} %bitcast.73), channel_id=1, replica_groups=mesh['dp'=4,'expert'=8] {'dp'}, dimensions={0} | all-to-all | bytes 2359296 | tf_op jit(solution)/shard_map/all_to_all | solution.py:124
  131.0 1.2 convert_element_type.93
  132.2 0.3 multiply_convert_fusion.1
  132.6 1.7 collective-permute-start
  134.3 0.9 pad_maximum_fusion.3
  135.1 6.1 %collective-permute-done = bf16[1,192,768]{2,1,0:T(8,128)(2,1)S(1)} collective-permute-done((bf16[1,192,768]{2,1,0:T(8,128)(2,1)S(1)}, bf16[1,192,768]{2,1,0:T(8,128)(2,1)S(1)}, u32[]{:S(2)}, u32[]{:S(2)}) %collective-permute-start) | collective-permute-done | bytes 294944 | tf_op jit(solution)/shard_map/ppermute | solution.py:18
  141.4 1.8 collective-permute-start.1
  143.2 56.0 %collective-permute-done.1 = bf16[2,192,768]{2,1,0:T(8,128)(2,1)S(1)} collective-permute-done((bf16[2,192,768]{2,1,0:T(8,128)(2,1)S(1)}, bf16[2,192,768]{2,1,0:T(8,128)(2,1)S(1)}, u32[]{:S(2)}, u32[]{:S(2)}) %collective-permute-start.1) | collective-permute-done | bytes 589856 | tf_op jit(solution)/shard_map/ppermute | solution.py:18
  199.6 7.2 %convolution_convert_fusion.3 = bf16[8,96,1024]{2,1,0:T(8,128)(2,1)S(1)} fusion(bf16[8,96,768]{2,1,0:T(8,128)(2,1)S(1)} %bitcast.64, bf16[8,768,1024]{2,1,0:T(8,128)(2,1)} %param.15), kind=kOutput, calls=%fused_computation.16 | convolution fusion | flops 1208745984 | bytes 15335424 | tf_op jit(solution)/shard_map/jrf,jfd->jrd/dot_general | solution.py:145
  206.8 0.9 copy.68
  207.7 0.9 copy.69
  208.6 2.0 copy.70
  210.6 4.6 %all-to-all-start.1 = ((bf16[8,96,1024]{2,1,0:T(8,128)(2,1)}), bf16[8,96,1024]{2,1,0:T(8,128)(2,1)S(1)}, u32[]{:S(2)}, u32[]{:S(2)}) async-start(bf16[8,96,1024]{2,1,0:T(8,128)(2,1)} %copy.70), calls=%async_computation.2 | async-start | bytes 3145728 | tf_op jit(solution)/shard_map/all_to_all | solution.py:151
  215.5 0.2 convert_reduce_fusion.2
  216.2 10.0 %convolution_convert_fusion = bf16[8,768,1024]{2,1,0:T(8,128)(2,1)} fusion(bf16[8,96,768]{2,1,0:T(8,128)(2,1)} %bitcast.65, bf16[8,96,1024]{2,1,0:T(8,128)(2,1)} %bitcast.59), kind=kOutput, calls=%fused_computation.5 | convolution fusion | flops 1214251008 | bytes 15335424 | tf_op jit(solution)/shard_map/jrf,jrd->jfd/dot_general | solution.py:158
  226.2 10.1 %all-to-all-done.1 = bf16[8,96,1024]{2,1,0:T(8,128)(2,1)S(1)} async-done(((bf16[8,96,1024]{2,1,0:T(8,128)(2,1)}), bf16[8,96,1024]{2,1,0:T(8,128)(2,1)S(1)}, u32[]{:S(2)}, u32[]{:S(2)}) %all-to-all-start.1) | async-done | bytes 1572896 | tf_op jit(solution)/shard_map/all_to_all | solution.py:151
  236.3 2.7 gather_fusion
  239.0 1.8 fusion.13
  240.8 9.3 %fusion.14 = f32[8,96,1024]{2,1,0:T(8,128)S(1)} fusion(bf16[8,96,768]{2,1,0:T(8,128)(2,1)S(1)} %bitcast.60, bf16[8,1024,768]{2,1,0:T(8,128)(2,1)} %param.13), kind=kOutput, calls=%fused_computation.64 | convolution fusion | flops 1207959552 | bytes 16908288 | tf_op jit(solution)/shard_map/jrf,jdf->jrd/dot_general | solution.py:162
  250.1 8.5 %add_convert_fusion = bf16[8,96,1024]{2,1,0:T(8,128)(2,1)S(1)} fusion(f32[8,96,1024]{2,1,0:T(8,128)S(1)} %fusion.14, bf16[8,96,768]{2,1,0:T(8,128)(2,1)S(1)} %bitcast.62, bf16[8,1024,768]{2,1,0:T(8,128)(2,1)} %param.14), kind=kOutput, calls=%fused_computation.12 | convolution fusion | flops 1209532416 | bytes 18481152 | tf_op jit(solution)/shard_map/jrf,jdf->jrd/dot_general | solution.py:168
  258.6 0.9 copy.74
  259.5 0.9 copy.75
  260.3 2.0 copy.76
  262.3 3.8 %all-to-all-start.3 = ((bf16[8,96,1024]{2,1,0:T(8,128)(2,1)}), bf16[8,96,1024]{2,1,0:T(8,128)(2,1)S(1)}, u32[]{:S(2)}, u32[]{:S(2)}) async-start(bf16[8,96,1024]{2,1,0:T(8,128)(2,1)} %copy.76), calls=%async_computation.4 | async-start | bytes 3145728 | tf_op jit(solution)/shard_map/all_to_all | solution.py:178
  266.2 2.4 multiply_reduce_fusion
  268.6 8.0 %convolution_convert_fusion.1 = bf16[8,1024,768]{2,1,0:T(8,128)(2,1)} fusion(bf16[8,96,1024]{2,1,0:T(8,128)(2,1)S(1)} %bitcast.54, bf16[8,96,768]{2,1,0:T(8,128)(2,1)} %bitcast.63), kind=kOutput, calls=%fused_computation.6 | convolution fusion | flops 1214251008 | bytes 15335424 | tf_op jit(solution)/shard_map/jrd,jrf->jdf/dot_general | solution.py:188
  276.6 6.6 %convolution_convert_fusion.2 = bf16[8,1024,768]{2,1,0:T(8,128)(2,1)} fusion(bf16[8,96,1024]{2,1,0:T(8,128)(2,1)S(1)} %bitcast.55, bf16[8,96,768]{2,1,0:T(8,128)(2,1)S(1)} %bitcast.61), kind=kOutput, calls=%fused_computation.7 | convolution fusion | flops 1214251008 | bytes 15335424 | tf_op jit(solution)/shard_map/jrd,jrf->jdf/dot_general | solution.py:185
  283.2 3.7 %all-to-all-done.3 = bf16[8,96,1024]{2,1,0:T(8,128)(2,1)S(1)} async-done(((bf16[8,96,1024]{2,1,0:T(8,128)(2,1)}), bf16[8,96,1024]{2,1,0:T(8,128)(2,1)S(1)}, u32[]{:S(2)}, u32[]{:S(2)}) %all-to-all-start.3) | async-done | bytes 1572896 | tf_op jit(solution)/shard_map/all_to_all | solution.py:178
  286.9 2.1 gather_fusion.1
  289.0 1.1 fusion.3
  (56 shorter events, 3.0 us)
Async XLA Ops:
  11.3 27.3 %all-to-all-start = ((bf16[8,48,2176]{2,1,0:T(8,128)(2,1)}), bf16[8,48,2176]{2,1,0:T(8,128)(2,1)S(1)}, u32[]{:S(2)}, u32[]{:S(2)}) async-start(bf16[8,48,2176]{2,1,0:T(8,128)(2,1)} %broadcast_in_dim.63), calls=%async_computation | async-start | bytes 3342336 | tf_op jit(solution)/shard_map/all_to_all | solution.py:69
  16.5 114.5 %reduce-scatter.2.cloned.1.call-start = ((), (), s32[]{:S(2)}) async-start(), calls=%async_computation.5 | async-start | bytes 2949120 | tf_op jit(solution)/shard_map/reduce_scatter | solution.py:119
  42.2 6.9 %copy-start = (bf16[8,1024,768]{2,1,0:T(8,128)(2,1)S(1)}, bf16[8,1024,768]{2,1,0:T(8,128)(2,1)}, u32[]{:S(2)}) copy-start(bf16[8,1024,768]{2,1,0:T(8,128)(2,1)} %param.14) | copy-start | bytes 37748740
  44.1 3.2 %copy-start.1 = (f32[768,2048]{1,0:T(8,128)}, f32[768,2048]{1,0:T(8,128)S(1)}, u32[]{:S(2)}) copy-start(f32[768,2048]{1,0:T(8,128)S(1)} %fusion.1) | copy-start | bytes 18874372
  59.3 179.7 %all-gather.2.cloned.1.call-start = ((), (), s32[]{:S(2)}) async-start(), calls=%async_computation.6 | async-start | bytes 2949120 | tf_op jit(solution)/shard_map/all_gather | solution.py:136
  63.0 9.6 %copy-start.2 = (bf16[768,1024]{1,0:T(8,128)(2,1)}, bf16[768,1024]{1,0:T(8,128)(2,1)S(1)}, u32[]{:S(2)}) copy-start(bf16[768,1024]{1,0:T(8,128)(2,1)S(1)} %fusion) | copy-start | bytes 4718596
  132.6 8.7 %collective-permute-start = (bf16[1,192,768]{2,1,0:T(8,128)(2,1)S(1)}, bf16[1,192,768]{2,1,0:T(8,128)(2,1)S(1)}, u32[]{:S(2)}, u32[]{:S(2)}) collective-permute-start(bf16[1,192,768]{2,1,0:T(8,128)(2,1)S(1)} %bitcast.74), channel_id=1, source_target_pairs={{0,8},{8,0},{16,24},{24,16},{1,9},{9,1},{17,25},{25,17},{2,10},{10... | collective-permute-start | bytes 884744 | tf_op jit(solution)/shard_map/ppermute | solution.py:18
  141.4 57.8 %collective-permute-start.1 = (bf16[2,192,768]{2,1,0:T(8,128)(2,1)S(1)}, bf16[2,192,768]{2,1,0:T(8,128)(2,1)S(1)}, u32[]{:S(2)}, u32[]{:S(2)}) collective-permute-start(bf16[2,192,768]{2,1,0:T(8,128)(2,1)S(1)} %get-tuple-element.14), channel_id=1, source_target_pairs={{0,16},{8,24},{16,0},{24,8},{1,17},{9,25},{17,1},{25,9},{2,18},{10... | collective-permute-start | bytes 1769480 | tf_op jit(solution)/shard_map/ppermute | solution.py:18
  199.6 7.3 %copy-start.6 = (bf16[2,2,192,768]{3,2,1,0:T(8,128)(2,1)}, bf16[2,2,192,768]{3,2,1,0:T(8,128)(2,1)S(1)}, u32[]{:S(2)}) copy-start(bf16[2,2,192,768]{3,2,1,0:T(8,128)(2,1)S(1)} %reverse_select_fusion) | copy-start | bytes 3538948
  210.6 4.7 %copy-start.8 = (f32[48,8]{0,1:T(8,128)S(1)}, f32[48,8]{0,1:T(8,128)}, u32[]{:S(2)}) copy-start(f32[48,8]{0,1:T(8,128)} %param.12) | copy-start | bytes 4612
  210.6 4.7 %copy-start.7 = (s32[48,8]{0,1:T(8,128)S(1)}, s32[48,8]{0,1:T(8,128)}, u32[]{:S(2)}) copy-start(s32[48,8]{0,1:T(8,128)} %param.11) | copy-start | bytes 4612
  210.6 25.7 %all-to-all-start.1 = ((bf16[8,96,1024]{2,1,0:T(8,128)(2,1)}), bf16[8,96,1024]{2,1,0:T(8,128)(2,1)S(1)}, u32[]{:S(2)}, u32[]{:S(2)}) async-start(bf16[8,96,1024]{2,1,0:T(8,128)(2,1)} %copy.70), calls=%async_computation.2 | async-start | bytes 3145728 | tf_op jit(solution)/shard_map/all_to_all | solution.py:151
  240.7 9.3 %copy-start.3 = (bf16[768,768]{1,0:T(8,128)(2,1)}, bf16[768,768]{1,0:T(8,128)(2,1)S(1)}, u32[]{:S(2)}) copy-start(bf16[768,768]{1,0:T(8,128)(2,1)S(1)} %get-tuple-element.9) | copy-start | bytes 3538948
  240.8 9.3 %copy-start.5 = (bf16[768,768]{1,0:T(8,128)(2,1)}, bf16[768,768]{1,0:T(8,128)(2,1)S(1)}, u32[]{:S(2)}) copy-start(bf16[768,768]{1,0:T(8,128)(2,1)S(1)} %get-tuple-element.8) | copy-start | bytes 3538948
  262.3 24.5 %all-to-all-start.3 = ((bf16[8,96,1024]{2,1,0:T(8,128)(2,1)}), bf16[8,96,1024]{2,1,0:T(8,128)(2,1)S(1)}, u32[]{:S(2)}, u32[]{:S(2)}) async-start(bf16[8,96,1024]{2,1,0:T(8,128)(2,1)} %copy.76), calls=%async_computation.4 | async-start | bytes 3145728 | tf_op jit(solution)/shard_map/all_to_all | solution.py:178
  268.6 8.0 %copy-start.4 = (bf16[768,768]{1,0:T(8,128)(2,1)S(1)}, bf16[768,768]{1,0:T(8,128)(2,1)}, u32[]{:S(2)}) copy-start(bf16[768,768]{1,0:T(8,128)(2,1)} %copy-done.3) | copy-start | bytes 3538948
Sparse Core Ops, SparseCore 0:
  59.4 66.0 reduce-scatter.1
  135.3 72.2 all-gather.1
